TPU v7x, 128 devices: a whole 4x4x4 slice. The times are simulated.
128 devices in a mesh: dp: 16 (over x, y_lo, core), tensor: 8 (over z, y_hi).
Axes of the slice: x: 4, y: 4 (y_hi: 2, y_lo: 2; y = y_hi * 2 + y_lo), z: 4, core: 2. Of those that a mesh axis runs over, the one named last changes fastest.
Arguments:
- rows_in: bfloat16 [2048, 6144], P('dp'), may hold values from -6 to 6
- out_grad: bfloat16 [2048, 6144], P('dp'), may hold values from -1.5 to 1.5
- gate_pre: bfloat16 [2048, 12288], P('dp', 'tensor'), may hold values from -5 to 5
- up_pre: bfloat16 [2048, 12288], P('dp', 'tensor'), may hold values from -5 to 5
- w_gate: bfloat16 [2, 6144, 12288], P(None, 'dp', 'tensor'), may hold values from -0.078125 to 0.078125
- w_up: bfloat16 [2, 6144, 12288], P(None, 'dp', 'tensor'), may hold values from -0.078125 to 0.078125
- w_down: bfloat16 [2, 12288, 6144], P(None, 'tensor', 'dp'), may hold values from -0.0546875 to 0.0546875
- live_rows: int32 [16], P('dp'), may hold values from 32 to 128, as said below
- block_expert: int32 [16], replicated, may hold values from 0 to 1, as said below
Outputs:
- input_grad: bfloat16 [2048, 6144], P('dp', 'tensor')
- grad_gate: bfloat16 [2, 6144, 12288], P(None, 'dp', 'tensor')
- grad_up: bfloat16 [2, 6144, 12288], P(None, 'dp', 'tensor')
- grad_down: bfloat16 [2, 12288, 6144], P(None, 'tensor', 'dp')
Inputs may be any that keep to these rules, and one draw needn't show every extreme that they name: `live_rows`: entry k counts the live rows among rank k's 128 rows; they come first and the rest are padding; some rank is full. `block_expert`: the expert of each aligned block of 128 rows; every expert owns at least one block.
All inputs are finite; a program needn't handle non-finite values.
Results may differ from a plain program's by a relative error of at most 0.005.
Values may be sent and summed in bfloat16 or wider, within the bound.
No kernel may reach another device: no remote copies, remote signals or barrier semaphores. Data moves between devices by JAX's collectives and lax.ppermute only.
A program may use at most 128 MiB of HBM per device.

v0:
```python
import numpy as np
import jax
import jax.numpy as jnp
from jax import lax
from jax.sharding import Mesh
from jax.sharding import PartitionSpec as P

BLOCK = 128
AXES = ("x", "ylo", "core", "z", "yhi")
SIZES = (4, 2, 2, 4, 2)
DP = ("x", "ylo", "core")
TP = ("z", "yhi")
CHIPS = ("x", "ylo")
N_DP = 16
N_TP = 8


def rank_of_pos(pos):
    core, x, ylo = (pos // 8, pos % 8 // 2, pos % 2)
    return x * 4 + ylo * 2 + core


POS_RANK = np.array([rank_of_pos(p) for p in range(N_DP)], np.int32)


def deliver_perm(k):
    pairs = []
    for i in range(N_DP):
        for t in range(N_TP):
            dest = 8 * (i % 2 ^ k) + t
            pairs.append((i * N_TP + t, dest * N_TP + i // 2))
    return pairs


def contract_rows(left_op, right_op):
    return lax.dot_general(
        left_op, right_op, (((0,), (0,)), ((), ())), preferred_element_type=jnp.float32
    )


def contract_cols(left_op, right_op):
    return lax.dot_general(
        left_op, right_op, (((1,), (1,)), ((), ())), preferred_element_type=jnp.float32
    )


def expert_masks(block_expert, row_count, expert_count):
    spread = jnp.broadcast_to(block_expert[:, None], (row_count // BLOCK, BLOCK)).reshape(
        row_count, 1
    )
    return [(spread == which).astype(jnp.bfloat16) for which in range(expert_count)]


def to_gathered_order(cols):
    width = cols.shape[1]
    return cols.reshape(4, 2, 2, BLOCK, width).transpose(2, 0, 1, 3, 4).reshape(-1, width)


def shards(rows_in, out_grad, gate_pre, up_pre, w_gate, w_up, w_down, live_rows, block_expert):
    rows_dev = rows_in.shape[0]
    expert_count = w_gate.shape[0]
    ff = gate_pre.shape[1]
    dy_cols = lax.all_to_all(out_grad, DP, split_axis=1, concat_axis=0, tiled=True)
    row_count = dy_cols.shape[0]
    expert_g = jnp.take(block_expert, jnp.asarray(POS_RANK), axis=0)
    masks_g = expert_masks(expert_g, row_count, expert_count)
    masks = expert_masks(block_expert, row_count, expert_count)
    positions = jnp.arange(rows_dev, dtype=jnp.int32)[:, None]
    row_mask = (positions < live_rows[0]).astype(jnp.float32)
    gate_vals = gate_pre.astype(jnp.float32)
    up_vals = up_pre.astype(jnp.float32)
    sigmoid = jax.nn.sigmoid(gate_vals)
    silu_vals = gate_vals * sigmoid
    hidden = (silu_vals * up_vals * row_mask).astype(jnp.bfloat16)
    hid_g = lax.all_gather(hidden, DP, axis=0, tiled=True)
    dy_g = to_gathered_order(dy_cols)
    result = jnp.zeros((row_count, ff), jnp.float32)
    for which in range(expert_count):
        result = result + contract_cols(dy_g * masks_g[which], w_down[which])
    hid_g, result = lax.optimization_barrier((hid_g, result))
    result = lax.psum_scatter(
        result.reshape(2, row_count // 2, ff), "core", scatter_dimension=0, tiled=True
    ).reshape(N_DP // 2, rows_dev, ff)
    pieces = lax.all_to_all(result, CHIPS, split_axis=0, concat_axis=0, tiled=True)
    hidden_grad = jnp.sum(pieces, axis=0)
    rows_in, hidden_grad = lax.optimization_barrier((rows_in, hidden_grad))
    x_cols = lax.all_to_all(rows_in, DP, split_axis=1, concat_axis=0, tiled=True)
    up_grad = (hidden_grad * silu_vals * row_mask).astype(jnp.bfloat16)
    gate_grad = (
        hidden_grad * up_vals * sigmoid * (1.0 + gate_vals * (1.0 - sigmoid)) * row_mask
    ).astype(jnp.bfloat16)
    packed = jnp.stack([gate_grad, up_grad], axis=1)
    packed = lax.all_gather(packed, DP, axis=0, tiled=True)
    gate_g, up_g = (packed[:, 0], packed[:, 1])
    down_terms = []
    gate_terms = []
    up_terms = []
    for which in range(expert_count):
        down_terms.append(contract_rows(hid_g * masks[which], dy_cols))
        gate_masked = gate_g * masks[which]
        up_masked = up_g * masks[which]
        gate_terms.append(contract_rows(x_cols, gate_masked))
        up_terms.append(contract_rows(x_cols, up_masked))
    down_total = jnp.stack(down_terms, 0)
    gate_total = jnp.stack(gate_terms, 0)
    up_total = jnp.stack(up_terms, 0)
    width = w_gate.shape[1]
    half_rows = row_count // 2
    summed = []
    for half in range(2):
        rows = slice(half * half_rows, (half + 1) * half_rows)
        partial_rows = jnp.zeros((half_rows, width), jnp.float32)
        for which in range(expert_count):
            gate_masked = gate_g[rows] * masks[which][rows]
            up_masked = up_g[rows] * masks[which][rows]
            partial_rows = (
                partial_rows
                + contract_cols(gate_masked, w_gate[which])
                + contract_cols(up_masked, w_up[which])
            )
        pieces = lax.all_to_all(
            partial_rows.reshape(N_TP, rows_dev, width), TP, split_axis=0, concat_axis=0, tiled=True
        )
        summed.append(jnp.sum(pieces, axis=0))
    summed = jnp.stack(summed, 0)
    core = lax.axis_index("core")
    low = lax.axis_index("x") < 2
    got = []
    for k in range(2):
        piece = lax.dynamic_index_in_dim(summed, core ^ k, 0, keepdims=False)
        got.append(lax.ppermute(piece, AXES, deliver_perm(k)))
    first = jnp.where(low, got[0], got[1])
    second = jnp.where(low, got[1], got[0])
    input_grad = jnp.concatenate([first, second], axis=1).astype(jnp.bfloat16)
    return (
        input_grad,
        gate_total.astype(jnp.bfloat16),
        up_total.astype(jnp.bfloat16),
        down_total.astype(jnp.bfloat16),
    )


def solution(mesh):
    fine = Mesh(mesh.devices.reshape(SIZES), AXES)
    return jax.shard_map(
        shards,
        mesh=fine,
        in_specs=(
            P(DP, None),
            P(DP, None),
            P(DP, TP),
            P(DP, TP),
            P(None, DP, TP),
            P(None, DP, TP),
            P(None, TP, DP),
            P(DP),
            P(),
        ),
        out_specs=(P(DP, TP), P(None, DP, TP), P(None, DP, TP), P(None, TP, DP)),
        check_vma=False,
    )
```

profile of v0, /device:TPU:3, one launch (start us, length us, event | category | flops | bytes accessed | tf_op | source)
XLA Modules:
  0.0 359.7 jit_solution(13972185572916459537)
XLA Ops:
  8.0 2.1 fusion.128
  10.2 1.6 copy.16
  11.7 6.3 %all-to-all-start = ((bf16[128,16,384]{0,2,1:T(8,128)(2,1)}), bf16[128,16,384]{0,2,1:T(8,128)(2,1)S(1)}, u32[]{:S(2)}, u32[]{:S(2)}) async-start(bf16[128,16,384]{0,2,1:T(8,128)(2,1)} %bitcast.1), calls=%async_computation | async-start | bytes 3145728 | tf_op jit(solution)/shard_map/all_to_all | solution.py:63
  18.1 0.7 gather_fusion
  19.2 30.3 %all-to-all-done = bf16[128,16,384]{0,2,1:T(8,128)(2,1)S(1)} async-done(((bf16[128,16,384]{0,2,1:T(8,128)(2,1)}), bf16[128,16,384]{0,2,1:T(8,128)(2,1)S(1)}, u32[]{:S(2)}, u32[]{:S(2)}) %all-to-all-start) | async-done | bytes 1572896 | tf_op jit(solution)/shard_map/all_to_all | solution.py:63
  49.5 0.9 copy.17
  51.1 1.5 copy-done.1
  52.7 3.5 fusion.115
  56.1 6.7 %convolution_add_fusion = f32[2048,1536]{1,0:T(8,128)} fusion(f32[2048,1536]{1,0:T(8,128)S(1)} %fusion.115, bf16[2048,384]{1,0:T(8,128)(2,1)S(1)} %bitcast.142, bf16[2,1536,384]{2,1,0:T(8,128)(2,1)S(1)} %copy-done.1), kind=kOutput, calls=%fused_computation.1 | convolution fusion | flops 2419064832 | bytes 27918336 | tf_op jit(solution)/shard_map/dot_general | solution.py:42
  62.8 6.6 %all-gather.3.cloned.1.call-done = bf16[2048,1536]{1,0:T(8,128)(2,1)} async-done(((bf16[128,1536]{1,0:T(8,128)(2,1)}), bf16[2048,1536]{1,0:T(8,128)(2,1)}) %all-gather.3.cloned.1.call-update) | async-done | bytes 6291472 | tf_op jit(solution)/shard_map/all_gather | solution.py:75
  69.5 28.4 %reduce-scatter.2.cloned.1.call-done = f32[1,1024,1536]{2,1,0:T(8,128)} async-done(((f32[2,1024,1536]{2,1,0:T(8,128)}), f32[1,1024,1536]{2,1,0:T(8,128)}) %reduce-scatter.2.cloned.1.call-update) | async-done | bytes 6291472 | tf_op jit(solution)/shard_map/reduce_scatter | solution.py:81
  97.9 75.3 %all_to_all.53 = f32[8,128,1536]{2,1,0:T(8,128)} all-to-all(f32[8,128,1536]{2,1,0:T(8,128)} %bitcast.144), channel_id=1, replica_groups=mesh['x'=4,'ylo'=2,'core'=2,'z'=4,'yhi'=2] {'x','ylo'}, dimensions={0} | all-to-all | bytes 12582912 | tf_op jit(solution)/shard_map/all_to_all | solution.py:84
  173.2 3.4 reduce_sum.27
  176.7 0.5 fusion.138
  177.2 0.9 pad_maximum_fusion.3
  178.9 1.6 copy.22
  180.4 6.1 %all-to-all-start.4 = ((bf16[128,16,384]{0,2,1:T(8,128)(2,1)}), bf16[128,16,384]{0,2,1:T(8,128)(2,1)S(1)}, u32[]{:S(2)}, u32[]{:S(2)}) async-start(bf16[128,16,384]{0,2,1:T(8,128)(2,1)} %bitcast.36), calls=%async_computation.5 | async-start | bytes 3145728 | tf_op jit(solution)/shard_map/all_to_all | solution.py:87
  186.5 6.3 %fusion.88 = bf16[1,1536,384]{2,1,0:T(8,128)(2,1)S(1)} fusion(bf16[2048,384]{1,0:T(8,128)(2,1)S(1)} %bitcast.148, bf16[2048,1536]{1,0:T(8,128)(2,1)} %all-gather.3.cloned.1.call-done, bf16[2048]{0:T(1024)(128)(2,1)S(1)} %broadcast_bitcast_fusion), kind=kOutput, calls=%fused_computation.70 | convolution fusion | flops 2419654656 | bytes 9048064 | tf_op jit(solution)/shard_map/dot_general | solution.py:36
  192.8 6.3 %fusion.91 = bf16[1,1536,384]{2,1,0:T(8,128)(2,1)S(1)} fusion(bf16[2048,384]{1,0:T(8,128)(2,1)S(1)} %bitcast.149, bf16[2048,1536]{1,0:T(8,128)(2,1)} %all-gather.3.cloned.1.call-done, bf16[2048]{0:T(1024)(128)(2,1)S(1)} %broadcast_bitcast_fusion.1), kind=kOutput, calls=%fused_computation.71 | convolution fusion | flops 2419654656 | bytes 9048064 | tf_op jit(solution)/shard_map/dot_general | solution.py:36
  199.2 1.7 pad_maximum_fusion.2
  200.8 18.7 %all-to-all-done.4 = bf16[128,16,384]{0,2,1:T(8,128)(2,1)S(1)} async-done(((bf16[128,16,384]{0,2,1:T(8,128)(2,1)}), bf16[128,16,384]{0,2,1:T(8,128)(2,1)S(1)}, u32[]{:S(2)}, u32[]{:S(2)}) %all-to-all-start.4) | async-done | bytes 1572896 | tf_op jit(solution)/shard_map/all_to_all | solution.py:87
  219.5 1.6 copy.23
  221.1 45.7 %all-gather.5.cloned.1.call-done = bf16[2048,2,1536]{2,0,1:T(8,128)(2,1)} async-done(((bf16[128,2,1536]{2,0,1:T(8,128)(2,1)}), bf16[2048,2,1536]{2,0,1:T(8,128)(2,1)}) %all-gather.5.cloned.1.call-update) | async-done | bytes 12582928 | tf_op jit(solution)/shard_map/all_gather | solution.py:93
  266.8 4.2 %fusion.20 = f32[1024,384]{1,0:T(8,128)S(1)} fusion(bf16[2048,2,1536]{2,0,1:T(8,128)(2,1)} %all-gather.5.cloned.1.call-done, bf16[1024]{0:T(1024)(128)(2,1)S(1)} %broadcast_bitcast_fusion.2, bf16[2,384,1536]{2,1,0:T(8,128)(2,1)} %param.15), kind=kOutput, calls=%fused_computation.22 | convolution fusion | flops 1209532416 | bytes 5900288 | tf_op jit(solution)/shard_map/dot_general | solution.py:42
  271.0 1.7 copy-done.10
  272.6 1.8 fusion.24
  274.5 1.8 fusion.26
  276.3 3.0 add_add_fusion
  279.3 6.8 %all-to-all-start.3 = ((f32[8,128,384]{2,1,0:T(8,128)}), f32[8,128,384]{2,1,0:T(8,128)S(1)}, u32[]{:S(2)}, u32[]{:S(2)}) async-start(f32[8,128,384]{2,1,0:T(8,128)} %bitcast.32), calls=%async_computation.4 | async-start | bytes 3145728 | tf_op jit(solution)/shard_map/all_to_all | solution.py:121
  286.1 4.2 %fusion.32 = f32[1024,384]{1,0:T(8,128)S(1)} fusion(bf16[2048,2,1536]{2,0,1:T(8,128)(2,1)} %all-gather.5.cloned.1.call-done, bf16[1024]{0:T(1024)(128)(2,1)S(1)} %broadcast_bitcast_fusion.5, bf16[2,384,1536]{2,1,0:T(8,128)(2,1)} %param.15), kind=kOutput, calls=%fused_computation.34 | convolution fusion | flops 1209532416 | bytes 5900288 | tf_op jit(solution)/shard_map/dot_general | solution.py:42
  290.3 3.9 %fusion.34 = f32[1024,384]{1,0:T(8,128)S(1)} fusion(bf16[2048,2,1536]{2,0,1:T(8,128)(2,1)} %all-gather.5.cloned.1.call-done, bf16[1024]{0:T(1024)(128)(2,1)S(1)} %broadcast_bitcast_fusion.5, bf16[2,384,1536]{2,1,0:T(8,128)(2,1)S(1)} %copy-done.14), kind=kOutput, calls=%fused_computation.36 | convolution fusion | flops 1209532416 | bytes 5900288 | tf_op jit(solution)/shard_map/dot_general | solution.py:42
  294.3 2.7 fusion.82
  297.0 2.7 fusion.85
  299.8 1.6 pad_maximum_fusion
  301.4 0.9 copy-done.12
  302.3 1.8 fusion.28
  304.1 3.1 add_add_fusion.1
  307.2 1.2 all-to-all-done.3
  308.4 5.4 %all-to-all-start.2 = ((f32[8,128,384]{2,1,0:T(8,128)}), f32[8,128,384]{2,1,0:T(8,128)S(1)}, u32[]{:S(2)}, u32[]{:S(2)}) async-start(f32[8,128,384]{2,1,0:T(8,128)} %bitcast.154), calls=%async_computation.3 | async-start | bytes 3145728 | tf_op jit(solution)/shard_map/all_to_all | solution.py:121
  313.9 7.1 %fusion.76 = bf16[1,384,1536]{2,1,0:T(8,128)(2,1)} fusion(bf16[2048,384]{1,0:T(8,128)(2,1)} %bitcast.150, bf16[2048,2,1536]{2,0,1:T(8,128)(2,1)} %all-gather.5.cloned.1.call-done, bf16[2048]{0:T(1024)(128)(2,1)S(1)} %broadcast_bitcast_fusion), kind=kOutput, calls=%fused_computation.66 | convolution fusion | flops 2419654656 | bytes 9048064 | tf_op jit(solution)/shard_map/dot_general | solution.py:36
  321.0 6.5 %fusion.79 = bf16[1,384,1536]{2,1,0:T(8,128)(2,1)} fusion(bf16[2048,384]{1,0:T(8,128)(2,1)S(1)} %bitcast.153, bf16[2048,2,1536]{2,0,1:T(8,128)(2,1)} %all-gather.5.cloned.1.call-done, bf16[2048]{0:T(1024)(128)(2,1)S(1)} %broadcast_bitcast_fusion.1), kind=kOutput, calls=%fused_computation.67 | convolution fusion | flops 2419654656 | bytes 9048064 | tf_op jit(solution)/shard_map/dot_general | solution.py:36
  327.6 8.1 %all-to-all-done.2 = f32[8,128,384]{2,1,0:T(8,128)S(1)} async-done(((f32[8,128,384]{2,1,0:T(8,128)}), f32[8,128,384]{2,1,0:T(8,128)S(1)}, u32[]{:S(2)}, u32[]{:S(2)}) %all-to-all-start.2) | async-done | bytes 1572896 | tf_op jit(solution)/shard_map/all_to_all | solution.py:121
  335.8 3.6 collective-permute-start
  339.4 2.6 collective-permute-start.1
  342.0 2.9 pad_maximum_fusion.1
  344.9 4.6 %collective-permute-done = bf16[128,384]{1,0:T(8,128)(2,1)S(1)} collective-permute-done((bf16[128,384]{1,0:T(8,128)(2,1)S(1)}, bf16[128,384]{1,0:T(8,128)(2,1)S(1)}, u32[]{:S(2)}, u32[]{:S(2)}) %collective-permute-start) | collective-permute-done | bytes 98336 | tf_op jit(solution)/shard_map/ppermute | solution.py:131
  349.5 2.9 collective-permute-done.1
  352.5 0.7 pad_maximum_fusion.4
  (62 shorter events, 2.4 us)
Async XLA Ops:
  7.2 3.0 copy-start.2
  7.2 62.3 %all-gather.3.cloned.1.call-start = ((), (), s32[]{:S(2)}) async-start(), calls=%async_computation.6 | async-start | bytes 6684672 | tf_op jit(solution)/shard_map/all_gather | solution.py:75
  11.7 6.4 %copy-start.9 = (s32[16]{0:T(128)S(1)}, s32[16]{0:T(128)}, u32[]{:S(2)}) copy-start(s32[16]{0:T(128)} %constant.55) | copy-start | bytes 196
  11.7 6.4 %copy-start = (s32[16]{0:T(128)S(1)}, s32[16]{0:T(128)}, u32[]{:S(2)}) copy-start(s32[16]{0:T(128)} %param.18) | copy-start | bytes 196
  11.7 37.8 %all-to-all-start = ((bf16[128,16,384]{0,2,1:T(8,128)(2,1)}), bf16[128,16,384]{0,2,1:T(8,128)(2,1)S(1)}, u32[]{:S(2)}, u32[]{:S(2)}) async-start(bf16[128,16,384]{0,2,1:T(8,128)(2,1)} %bitcast.1), calls=%async_computation | async-start | bytes 3145728 | tf_op jit(solution)/shard_map/all_to_all | solution.py:63
  18.0 79.9 %reduce-scatter.2.cloned.1.call-start = ((), (), s32[]{:S(2)}) async-start(), calls=%async_computation.7 | async-start | bytes 18874368 | tf_op jit(solution)/shard_map/reduce_scatter | solution.py:81
  51.0 1.7 copy-start.1
  69.5 197.3 %all-gather.5.cloned.1.call-start = ((), (), s32[]{:S(2)}) async-start(), calls=%async_computation.8 | async-start | bytes 13369344 | tf_op jit(solution)/shard_map/all_gather | solution.py:93
  173.2 3.4 copy-start.6
  173.2 3.4 copy-start.7
  177.2 1.7 copy-start.3
  180.4 39.1 %all-to-all-start.4 = ((bf16[128,16,384]{0,2,1:T(8,128)(2,1)}), bf16[128,16,384]{0,2,1:T(8,128)(2,1)S(1)}, u32[]{:S(2)}, u32[]{:S(2)}) async-start(bf16[128,16,384]{0,2,1:T(8,128)(2,1)} %bitcast.36), calls=%async_computation.5 | async-start | bytes 3145728 | tf_op jit(solution)/shard_map/all_to_all | solution.py:87
  221.1 49.9 %copy-start.11 = (bf16[2,384,1536]{2,1,0:T(8,128)(2,1)S(1)}, bf16[2,384,1536]{2,1,0:T(8,128)(2,1)}, u32[]{:S(2)}) copy-start(bf16[2,384,1536]{2,1,0:T(8,128)(2,1)} %param.15) | copy-start | bytes 7077892
  266.8 5.9 %copy-start.10 = (bf16[2048,2,1536]{2,0,1:T(8,128)(2,1)S(1)}, bf16[2048,2,1536]{2,0,1:T(8,128)(2,1)}, u32[]{:S(2)}) copy-start(bf16[2048,2,1536]{2,0,1:T(8,128)(2,1)} %all-gather.5.cloned.1.call-done) | copy-start | bytes 37748740
  272.6 1.8 copy-start.13
  279.3 29.1 %all-to-all-start.3 = ((f32[8,128,384]{2,1,0:T(8,128)}), f32[8,128,384]{2,1,0:T(8,128)S(1)}, u32[]{:S(2)}, u32[]{:S(2)}) async-start(f32[8,128,384]{2,1,0:T(8,128)} %bitcast.32), calls=%async_computation.4 | async-start | bytes 3145728 | tf_op jit(solution)/shard_map/all_to_all | solution.py:121
  286.1 4.2 %copy-start.14 = (bf16[2,384,1536]{2,1,0:T(8,128)(2,1)S(1)}, bf16[2,384,1536]{2,1,0:T(8,128)(2,1)}, u32[]{:S(2)}) copy-start(bf16[2,384,1536]{2,1,0:T(8,128)(2,1)} %param.14) | copy-start | bytes 7077892
  286.1 8.2 %slice-start = ((s8[12582912]{0:T(1024)(128)(4,1)}), s8[4194304]{0:T(1024)(128)(4,1)S(1)}, s32[]{:S(2)}) async-start(s8[12582912]{0:T(1024)(128)(4,1)} %bitcast.157), calls=%async_computation.9 | async-start | bytes 8388608
  286.1 8.2 %slice-start.1 = ((s8[12582912]{0:T(1024)(128)(4,1)}), s8[4194304]{0:T(1024)(128)(4,1)S(1)}, s32[]{:S(2)}) async-start(s8[12582912]{0:T(1024)(128)(4,1)} %bitcast.157), calls=%async_computation.10 | async-start | bytes 8388608
  290.3 3.9 %copy-start.4 = (bf16[16,128,384]{2,1,0:T(8,128)(2,1)S(1)}, bf16[16,128,384]{2,1,0:T(8,128)(2,1)}, u32[]{:S(2)}) copy-start(bf16[16,128,384]{2,1,0:T(8,128)(2,1)} %copy.23) | copy-start | bytes 4718596
  290.3 4.0 %slice-start.2 = ((s8[12582912]{0:T(1024)(128)(4,1)}), s8[4194304]{0:T(1024)(128)(4,1)S(1)}, s32[]{:S(2)}) async-start(s8[12582912]{0:T(1024)(128)(4,1)} %bitcast.157), calls=%async_computation.11 | async-start | bytes 8388608
  299.8 2.5 copy-start.12
  308.4 27.2 %all-to-all-start.2 = ((f32[8,128,384]{2,1,0:T(8,128)}), f32[8,128,384]{2,1,0:T(8,128)S(1)}, u32[]{:S(2)}, u32[]{:S(2)}) async-start(f32[8,128,384]{2,1,0:T(8,128)} %bitcast.154), calls=%async_computation.3 | async-start | bytes 3145728 | tf_op jit(solution)/shard_map/all_to_all | solution.py:121
  313.9 7.1 %copy-start.5 = (bf16[16,128,384]{2,1,0:T(8,128)(2,1)S(1)}, bf16[16,128,384]{2,1,0:T(8,128)(2,1)}, u32[]{:S(2)}) copy-start(bf16[16,128,384]{2,1,0:T(8,128)(2,1)} %copy.23) | copy-start | bytes 4718596
  327.6 14.4 %copy-start.8 = (bf16[1,384,1536]{2,1,0:T(8,128)(2,1)S(1)}, bf16[1,384,1536]{2,1,0:T(8,128)(2,1)}, u32[]{:S(2)}) copy-start(bf16[1,384,1536]{2,1,0:T(8,128)(2,1)} %fusion.76) | copy-start | bytes 3538948
  335.8 13.7 %collective-permute-start = (bf16[128,384]{1,0:T(8,128)(2,1)S(1)}, bf16[128,384]{1,0:T(8,128)(2,1)S(1)}, u32[]{:S(2)}, u32[]{:S(2)}) collective-permute-start(bf16[128,384]{1,0:T(8,128)(2,1)S(1)} %get-tuple-element.18), channel_id=1, source_target_pairs={{0,0},{1,8},{2,16},{3,24},{4,32},{5,40},{6,48},{7,56},{8,64},{9,72... | collective-permute-start | bytes 294920 | tf_op jit(solution)/shard_map/ppermute | solution.py:131
  339.4 13.0 %collective-permute-start.1 = (bf16[128,384]{1,0:T(8,128)(2,1)S(1)}, bf16[128,384]{1,0:T(8,128)(2,1)S(1)}, u32[]{:S(2)}, u32[]{:S(2)}) collective-permute-start(bf16[128,384]{1,0:T(8,128)(2,1)S(1)} %get-tuple-element.19), channel_id=1, source_target_pairs={{0,64},{1,72},{2,80},{3,88},{4,96},{5,104},{6,112},{7,120},{8,0},{... | collective-permute-start | bytes 294920 | tf_op jit(solution)/shard_map/ppermute | solution.py:131
Sparse Core Ops, SparseCore 0:
  10.3 59.0 all-gather.2
  71.8 26.0 reduce-scatter.1
  178.3 88.4 all-gather.4
where the time goes:
time: 360 us
  waiting for transfers between devices  147 us (41%)
  blocking collectives  75.3 us (21%)
  matrix products  65.7 us (18%)
  starting transfers between devices  30.8 us (9%)
  between operations  14.8 us (4%)
  other arithmetic  14.5 us (4%)
  local copies, waits for them, and re-layouts  11.9 us (3%)
    all_to_all x1, blocking collectives, shards(): lax.all_to_all(result, CHIPS, split_axis=0, concat_axis=0, tiled=True)  75.3 us
    all_gather x1, waiting for transfers between devices, shards(): packed = lax.all_gather(packed, DP, axis=0, tiled=True)  45.7 us
    dot_general x10, matrix products, contract_cols(): lax.dot_general(left_op, right_op, (((1,), (1,)), ((), ())), preferred_el...  34 us
    dot_general x6, matrix products, contract_rows(): lax.dot_general(left_op, right_op, (((0,), (0,)), ((), ())), preferred_el...  31.7 us
    all_to_all x1, waiting for transfers between devices, shards(): lax.all_to_all(out_grad, DP, split_axis=1, concat_axis=0, tiled=True)  30.3 us
    reduce_scatter x1, waiting for transfers between devices, shards(): lax.psum_scatter(result.reshape(2, row_count // 2, ff), 'core', scatter_d...  28.4 us
    all_to_all x1, waiting for transfers between devices, shards(): lax.all_to_all(rows_in, DP, split_axis=1, concat_axis=0, tiled=True)  18.7 us
    all_to_all x2, starting transfers between devices, shards(): lax.all_to_all(partial_rows.reshape(N_TP, rows_dev, width), TP, split_axi...  12.2 us
  transfers between devices with their start and end apart: 9, of which 9 were waited for; matrix products, arithmetic and copies ran while one was open for 19% of the time, Pallas kernels for 0%

commit v1 on v0

--- a/solution.py
+++ b/solution.py
@@ -90,7 +90,12 @@
         hidden_grad * up_vals * sigmoid * (1.0 + gate_vals * (1.0 - sigmoid)) * row_mask
     ).astype(jnp.bfloat16)
     packed = jnp.stack([gate_grad, up_grad], axis=1)
-    packed = lax.all_gather(packed, DP, axis=0, tiled=True)
+    packed = jnp.concatenate(
+        lax.all_to_all(
+            jnp.stack(lax.axis_size(DP) * [packed], 0), concat_axis=0, axis_name=DP, split_axis=0
+        ),
+        0,
+    )
     gate_g, up_g = (packed[:, 0], packed[:, 1])
     down_terms = []
     gate_terms = []

time: 360 us -> 534 us (1.48)
  the two profiles are of different devices: /device:TPU:3 before, /device:TPU:12 now
where the time goes in v1:
time: 534 us; the launch traced here: 526 us
  waiting for transfers between devices  297 us (56%)
  blocking collectives  74.7 us (14%)
  matrix products  66.2 us (12%)
  starting transfers between devices  32.3 us (6%)
  local copies, waits for them, and re-layouts  22.1 us (4%)
  other arithmetic  18.1 us (3%)
  between operations  15.4 us (3%)
    all_to_all x1, waiting for transfers between devices, shards(): lax.all_to_all(jnp.stack(lax.axis_size(DP) * [packed], 0), concat_axis=0,...  186 us
    all_to_all x1, blocking collectives, shards(): lax.all_to_all(result, CHIPS, split_axis=0, concat_axis=0, tiled=True)  74.7 us
    dot_general x10, matrix products, contract_cols(): lax.dot_general(left_op, right_op, (((1,), (1,)), ((), ())), preferred_el...  33.4 us
    dot_general x6, matrix products, contract_rows(): lax.dot_general(left_op, right_op, (((0,), (0,)), ((), ())), preferred_el...  32.8 us
    all_to_all x1, waiting for transfers between devices, shards(): lax.all_to_all(out_grad, DP, split_axis=1, concat_axis=0, tiled=True)  30 us
    reduce_scatter x1, waiting for transfers between devices, shards(): lax.psum_scatter(result.reshape(2, row_count // 2, ff), 'core', scatter_d...  29.2 us
    all_to_all x2, waiting for transfers between devices, shards(): lax.all_to_all(partial_rows.reshape(N_TP, rows_dev, width), TP, split_axi...  19.6 us
    all_to_all x1, waiting for transfers between devices, shards(): lax.all_to_all(rows_in, DP, split_axis=1, concat_axis=0, tiled=True)  17.7 us
  transfers between devices with their start and end apart: 9, of which 9 were waited for; matrix products, arithmetic and copies ran while one was open for 12% of the time, Pallas kernels for 0%

profile of v1, /device:TPU:12, one launch (start us, length us, event | category | flops | bytes accessed | tf_op | source)
XLA Modules:
  0.0 525.8 jit_solution(10121381865216121143)
XLA Ops:
  8.0 2.1 fusion.128
  10.2 1.6 copy.26
  11.7 5.9 %all-to-all-start = ((bf16[128,16,384]{0,2,1:T(8,128)(2,1)}), bf16[128,16,384]{0,2,1:T(8,128)(2,1)S(1)}, u32[]{:S(2)}, u32[]{:S(2)}) async-start(bf16[128,16,384]{0,2,1:T(8,128)(2,1)} %bitcast.1), calls=%async_computation | async-start | bytes 3145728 | tf_op jit(solution)/shard_map/all_to_all | solution.py:63
  17.7 0.7 gather_fusion
  18.8 30.0 %all-to-all-done = bf16[128,16,384]{0,2,1:T(8,128)(2,1)S(1)} async-done(((bf16[128,16,384]{0,2,1:T(8,128)(2,1)}), bf16[128,16,384]{0,2,1:T(8,128)(2,1)S(1)}, u32[]{:S(2)}, u32[]{:S(2)}) %all-to-all-start) | async-done | bytes 1572896 | tf_op jit(solution)/shard_map/all_to_all | solution.py:63
  48.8 0.9 copy.27
  50.4 1.5 copy-done.2
  51.9 3.5 fusion.115
  55.4 6.7 %convolution_add_fusion = f32[2048,1536]{1,0:T(8,128)} fusion(f32[2048,1536]{1,0:T(8,128)S(1)} %fusion.115, bf16[2048,384]{1,0:T(8,128)(2,1)S(1)} %bitcast.155, bf16[2,1536,384]{2,1,0:T(8,128)(2,1)S(1)} %copy-done.2), kind=kOutput, calls=%fused_computation.1 | convolution fusion | flops 2419064832 | bytes 27918336 | tf_op jit(solution)/shard_map/dot_general | solution.py:42
  62.1 6.1 %all-gather.2.cloned.1.call-done = bf16[2048,1536]{1,0:T(8,128)(2,1)} async-done(((bf16[128,1536]{1,0:T(8,128)(2,1)}), bf16[2048,1536]{1,0:T(8,128)(2,1)}) %all-gather.2.cloned.1.call-update) | async-done | bytes 6291472 | tf_op jit(solution)/shard_map/all_gather | solution.py:75
  68.1 29.2 %reduce-scatter.2.cloned.1.call-done = f32[1,1024,1536]{2,1,0:T(8,128)} async-done(((f32[2,1024,1536]{2,1,0:T(8,128)}), f32[1,1024,1536]{2,1,0:T(8,128)}) %reduce-scatter.2.cloned.1.call-update) | async-done | bytes 6291472 | tf_op jit(solution)/shard_map/reduce_scatter | solution.py:81
  97.4 74.7 %all_to_all.58 = f32[8,128,1536]{2,1,0:T(8,128)} all-to-all(f32[8,128,1536]{2,1,0:T(8,128)} %bitcast.157), channel_id=1, replica_groups=mesh['x'=4,'ylo'=2,'core'=2,'z'=4,'yhi'=2] {'x','ylo'}, dimensions={0} | all-to-all | bytes 12582912 | tf_op jit(solution)/shard_map/all_to_all | solution.py:84
  172.1 4.3 reduce_sum.27
  176.4 1.6 copy.33
  178.0 6.9 %all-to-all-start.5 = ((bf16[128,16,384]{0,2,1:T(8,128)(2,1)}), bf16[128,16,384]{0,2,1:T(8,128)(2,1)S(1)}, u32[]{:S(2)}, u32[]{:S(2)}) async-start(bf16[128,16,384]{0,2,1:T(8,128)(2,1)} %bitcast.37), calls=%async_computation.6 | async-start | bytes 3145728 | tf_op jit(solution)/shard_map/all_to_all | solution.py:87
  184.9 1.7 fusion.138
  186.6 0.9 pad_maximum_fusion.3
  187.6 17.7 %all-to-all-done.5 = bf16[128,16,384]{0,2,1:T(8,128)(2,1)S(1)} async-done(((bf16[128,16,384]{0,2,1:T(8,128)(2,1)}), bf16[128,16,384]{0,2,1:T(8,128)(2,1)S(1)}, u32[]{:S(2)}, u32[]{:S(2)}) %all-to-all-start.5) | async-done | bytes 1572896 | tf_op jit(solution)/shard_map/all_to_all | solution.py:87
  205.3 7.1 %stack.76 = bf16[16,128,2,1536]{3,1,2,0:T(8,128)(2,1)} broadcast(bf16[128,2,1536]{2,0,1:T(8,128)(2,1)} %pad_maximum_fusion.3), dimensions={1,2,3} | broadcast | bytes 13369344 | tf_op jit(solution)/shard_map/stack | solution.py:95
  212.4 7.2 %all-to-all-start.2 = ((bf16[16,128,2,1536]{3,1,2,0:T(8,128)(2,1)}), bf16[16,128,2,1536]{3,1,2,0:T(8,128)(2,1)}, u32[]{:S(2)}, u32[]{:S(2)}) async-start(bf16[16,128,2,1536]{3,1,2,0:T(8,128)(2,1)} %stack.76), calls=%async_computation.3 | async-start | bytes 25165824 | tf_op jit(solution)/shard_map/all_to_all | solution.py:94
  220.2 6.4 %fusion.88 = bf16[1,1536,384]{2,1,0:T(8,128)(2,1)S(1)} fusion(bf16[2048,384]{1,0:T(8,128)(2,1)S(1)} %bitcast.161, bf16[2048,1536]{1,0:T(8,128)(2,1)} %all-gather.2.cloned.1.call-done, bf16[2048]{0:T(1024)(128)(2,1)S(1)} %broadcast_bitcast_fusion), kind=kOutput, calls=%fused_computation.70 | convolution fusion | flops 2419654656 | bytes 9048064 | tf_op jit(solution)/shard_map/dot_general | solution.py:36
  226.5 6.3 %fusion.91 = bf16[1,1536,384]{2,1,0:T(8,128)(2,1)S(1)} fusion(bf16[2048,384]{1,0:T(8,128)(2,1)S(1)} %bitcast.162, bf16[2048,1536]{1,0:T(8,128)(2,1)} %all-gather.2.cloned.1.call-done, bf16[2048]{0:T(1024)(128)(2,1)S(1)} %broadcast_bitcast_fusion.1), kind=kOutput, calls=%fused_computation.71 | convolution fusion | flops 2419654656 | bytes 9048064 | tf_op jit(solution)/shard_map/dot_general | solution.py:36
  232.9 1.7 pad_maximum_fusion.2
  234.6 0.9 copy.34
  235.4 185.7 %all-to-all-done.2 = bf16[16,128,2,1536]{3,1,2,0:T(8,128)(2,1)} async-done(((bf16[16,128,2,1536]{3,1,2,0:T(8,128)(2,1)}), bf16[16,128,2,1536]{3,1,2,0:T(8,128)(2,1)}, u32[]{:S(2)}, u32[]{:S(2)}) %all-to-all-start.2) | async-done | bytes 12582944 | tf_op jit(solution)/shard_map/all_to_all | solution.py:94
  421.1 6.6 %copy.32 = bf16[16,128,2,1536]{3,1,0,2:T(8,128)(2,1)S(1)} copy(bf16[16,128,2,1536]{3,1,2,0:T(8,128)(2,1)} %all-to-all-done.2) | data formatting | bytes 25165824 | tf_op jit(solution)/shard_map/all_to_all | solution.py:94
  427.7 2.7 fusion.82
  430.5 3.7 fusion.85
  434.2 1.8 fusion.24
  436.1 1.8 fusion.26
  437.9 3.0 fusion.32
  440.9 3.0 fusion.34
  443.8 1.8 fusion.20
  445.7 3.1 add_add_fusion
  448.8 6.7 %all-to-all-start.4 = ((f32[8,128,384]{2,1,0:T(8,128)}), f32[8,128,384]{2,1,0:T(8,128)S(1)}, u32[]{:S(2)}, u32[]{:S(2)}) async-start(f32[8,128,384]{2,1,0:T(8,128)} %bitcast.33), calls=%async_computation.5 | async-start | bytes 3145728 | tf_op jit(solution)/shard_map/all_to_all | solution.py:126
  455.5 3.0 pad_maximum_fusion
  458.5 3.9 fusion.28
  462.4 4.9 add_add_fusion.1
  467.3 11.2 %all-to-all-done.4 = f32[8,128,384]{2,1,0:T(8,128)S(1)} async-done(((f32[8,128,384]{2,1,0:T(8,128)}), f32[8,128,384]{2,1,0:T(8,128)S(1)}, u32[]{:S(2)}, u32[]{:S(2)}) %all-to-all-start.4) | async-done | bytes 1572896 | tf_op jit(solution)/shard_map/all_to_all | solution.py:126
  478.6 3.6 all-to-all-start.3
  482.2 7.1 %fusion.76 = bf16[1,384,1536]{2,1,0:T(8,128)(2,1)} fusion(bf16[2048,384]{1,0:T(8,128)(2,1)} %bitcast.165, bf16[2048,2,1536]{2,0,1:T(8,128)(2,1)} %bitcast.153, bf16[2048]{0:T(1024)(128)(2,1)S(1)} %broadcast_bitcast_fusion), kind=kOutput, calls=%fused_computation.66 | convolution fusion | flops 2419654656 | bytes 9048064 | tf_op jit(solution)/shard_map/dot_general | solution.py:36
  489.3 6.5 %fusion.79 = bf16[1,384,1536]{2,1,0:T(8,128)(2,1)} fusion(bf16[2048,384]{1,0:T(8,128)(2,1)S(1)} %bitcast.166, bf16[2048,2,1536]{2,0,1:T(8,128)(2,1)} %bitcast.154, bf16[2048]{0:T(1024)(128)(2,1)S(1)} %broadcast_bitcast_fusion.1), kind=kOutput, calls=%fused_computation.67 | convolution fusion | flops 2419654656 | bytes 9048064 | tf_op jit(solution)/shard_map/dot_general | solution.py:36
  495.9 8.4 %all-to-all-done.3 = f32[8,128,384]{2,1,0:T(8,128)S(1)} async-done(((f32[8,128,384]{2,1,0:T(8,128)}), f32[8,128,384]{2,1,0:T(8,128)S(1)}, u32[]{:S(2)}, u32[]{:S(2)}) %all-to-all-start.3) | async-done | bytes 1572896 | tf_op jit(solution)/shard_map/all_to_all | solution.py:126
  504.5 1.9 collective-permute-start
  506.5 2.9 pad_maximum_fusion.1
  509.4 7.5 %collective-permute-done = bf16[128,384]{1,0:T(8,128)(2,1)S(1)} collective-permute-done((bf16[128,384]{1,0:T(8,128)(2,1)S(1)}, bf16[128,384]{1,0:T(8,128)(2,1)S(1)}, u32[]{:S(2)}, u32[]{:S(2)}) %collective-permute-start) | collective-permute-done | bytes 98336 | tf_op jit(solution)/shard_map/ppermute | solution.py:136
  516.8 1.1 collective-permute-done.1
  518.0 0.7 pad_maximum_fusion.4
  (58 shorter events, 2.3 us)
Async XLA Ops:
  7.2 3.0 copy-start.3
  7.2 60.9 %all-gather.2.cloned.1.call-start = ((), (), s32[]{:S(2)}) async-start(), calls=%async_computation.7 | async-start | bytes 6684672 | tf_op jit(solution)/shard_map/all_gather | solution.py:75
  11.7 5.9 %copy-start.9 = (s32[16]{0:T(128)S(1)}, s32[16]{0:T(128)}, u32[]{:S(2)}) copy-start(s32[16]{0:T(128)} %constant.55) | copy-start | bytes 196
  11.7 5.9 %copy-start = (s32[16]{0:T(128)S(1)}, s32[16]{0:T(128)}, u32[]{:S(2)}) copy-start(s32[16]{0:T(128)} %param.18) | copy-start | bytes 196
  11.7 37.1 %all-to-all-start = ((bf16[128,16,384]{0,2,1:T(8,128)(2,1)}), bf16[128,16,384]{0,2,1:T(8,128)(2,1)S(1)}, u32[]{:S(2)}, u32[]{:S(2)}) async-start(bf16[128,16,384]{0,2,1:T(8,128)(2,1)} %bitcast.1), calls=%async_computation | async-start | bytes 3145728 | tf_op jit(solution)/shard_map/all_to_all | solution.py:63
  17.6 79.8 %reduce-scatter.2.cloned.1.call-start = ((), (), s32[]{:S(2)}) async-start(), calls=%async_computation.8 | async-start | bytes 18874368 | tf_op jit(solution)/shard_map/reduce_scatter | solution.py:81
  50.2 1.7 copy-start.2
  172.1 4.4 copy-start.4
  178.0 6.9 %copy-start.7 = (bf16[128,1536]{1,0:T(8,128)(2,1)S(1)}, bf16[128,1536]{1,0:T(8,128)(2,1)}, u32[]{:S(2)}) copy-start(bf16[128,1536]{1,0:T(8,128)(2,1)} %param.12) | copy-start | bytes 1179652
  178.0 27.3 %all-to-all-start.5 = ((bf16[128,16,384]{0,2,1:T(8,128)(2,1)}), bf16[128,16,384]{0,2,1:T(8,128)(2,1)S(1)}, u32[]{:S(2)}, u32[]{:S(2)}) async-start(bf16[128,16,384]{0,2,1:T(8,128)(2,1)} %bitcast.37), calls=%async_computation.6 | async-start | bytes 3145728 | tf_op jit(solution)/shard_map/all_to_all | solution.py:87
  212.4 208.7 %all-to-all-start.2 = ((bf16[16,128,2,1536]{3,1,2,0:T(8,128)(2,1)}), bf16[16,128,2,1536]{3,1,2,0:T(8,128)(2,1)}, u32[]{:S(2)}, u32[]{:S(2)}) async-start(bf16[16,128,2,1536]{3,1,2,0:T(8,128)(2,1)} %stack.76), calls=%async_computation.3 | async-start | bytes 25165824 | tf_op jit(solution)/shard_map/all_to_all | solution.py:94
  235.4 195.0 %copy-start.5 = (bf16[16,128,384]{2,1,0:T(8,128)(2,1)}, bf16[16,128,384]{2,1,0:T(8,128)(2,1)S(1)}, u32[]{:S(2)}) copy-start(bf16[16,128,384]{2,1,0:T(8,128)(2,1)S(1)} %copy.34) | copy-start | bytes 4718596
  427.7 18.0 %copy-start.1 = (bf16[16,128,2,1536]{3,1,0,2:T(8,128)(2,1)}, bf16[16,128,2,1536]{3,1,0,2:T(8,128)(2,1)S(1)}, u32[]{:S(2)}) copy-start(bf16[16,128,2,1536]{3,1,0,2:T(8,128)(2,1)S(1)} %copy.32) | copy-start | bytes 37748740
  430.5 3.8 copy-start.10
  434.2 1.8 copy-start.12
  448.8 29.8 %all-to-all-start.4 = ((f32[8,128,384]{2,1,0:T(8,128)}), f32[8,128,384]{2,1,0:T(8,128)S(1)}, u32[]{:S(2)}, u32[]{:S(2)}) async-start(f32[8,128,384]{2,1,0:T(8,128)} %bitcast.33), calls=%async_computation.5 | async-start | bytes 3145728 | tf_op jit(solution)/shard_map/all_to_all | solution.py:126
  455.5 3.1 copy-start.11
  458.5 3.9 copy-start.13
  458.5 3.9 copy-start.14
  458.5 3.9 copy-start.15
  478.6 25.7 %all-to-all-start.3 = ((f32[8,128,384]{2,1,0:T(8,128)}), f32[8,128,384]{2,1,0:T(8,128)S(1)}, u32[]{:S(2)}, u32[]{:S(2)}) async-start(f32[8,128,384]{2,1,0:T(8,128)} %bitcast.167), calls=%async_computation.4 | async-start | bytes 3145728 | tf_op jit(solution)/shard_map/all_to_all | solution.py:126
  482.1 7.1 %copy-start.6 = (bf16[16,128,384]{2,1,0:T(8,128)(2,1)S(1)}, bf16[16,128,384]{2,1,0:T(8,128)(2,1)}, u32[]{:S(2)}) copy-start(bf16[16,128,384]{2,1,0:T(8,128)(2,1)} %copy-done.5) | copy-start | bytes 4718596
  495.9 10.6 %copy-start.8 = (bf16[1,384,1536]{2,1,0:T(8,128)(2,1)S(1)}, bf16[1,384,1536]{2,1,0:T(8,128)(2,1)}, u32[]{:S(2)}) copy-start(bf16[1,384,1536]{2,1,0:T(8,128)(2,1)} %fusion.76) | copy-start | bytes 3538948
  504.5 12.4 %collective-permute-start = (bf16[128,384]{1,0:T(8,128)(2,1)S(1)}, bf16[128,384]{1,0:T(8,128)(2,1)S(1)}, u32[]{:S(2)}, u32[]{:S(2)}) collective-permute-start(bf16[128,384]{1,0:T(8,128)(2,1)S(1)} %get-tuple-element.18), channel_id=1, source_target_pairs={{0,0},{1,8},{2,16},{3,24},{4,32},{5,40},{6,48},{7,56},{8,64},{9,72... | collective-permute-start | bytes 294920 | tf_op jit(solution)/shard_map/ppermute | solution.py:136
  506.4 11.6 %collective-permute-start.1 = (bf16[128,384]{1,0:T(8,128)(2,1)S(1)}, bf16[128,384]{1,0:T(8,128)(2,1)S(1)}, u32[]{:S(2)}, u32[]{:S(2)}) collective-permute-start(bf16[128,384]{1,0:T(8,128)(2,1)S(1)} %get-tuple-element.19), channel_id=1, source_target_pairs={{0,64},{1,72},{2,80},{3,88},{4,96},{5,104},{6,112},{7,120},{8,0},{... | collective-permute-start | bytes 294920 | tf_op jit(solution)/shard_map/ppermute | solution.py:136
Sparse Core Ops, SparseCore 0:
  10.3 57.7 all-gather.1
  70.5 26.7 reduce-scatter.1
